TPU v7x, 256 devices: a whole 4x4x8 slice. The times are simulated.
256 devices in a mesh: segment: 4 (over y), ctx: 32 (over x_hi, z, core), tp: 2 (over x_lo).
Axes of the slice: x: 4 (x_hi: 2, x_lo: 2; x = x_hi * 2 + x_lo), y: 4, z: 8, core: 2. Of those that a mesh axis runs over, the one named last changes fastest.
Arguments:
- held: bfloat16 [4, 8192, 3584], P('segment', 'ctx'), may hold values from -6 to 6
- text: bfloat16 [8192, 3584], P('ctx'), may hold values from -6 to 6
- frames: bfloat16 [4096, 1024], P('ctx'), may hold values from -6 to 6
- join: int32 [64], P('ctx'), may hold values from 0 to 8128, as said below
- ln_gain: float32 [1024], replicated, may hold values from 0.1 to 1.9
- w_proj: bfloat16 [1024, 3584], P('tp'), may hold values from -0.1875 to 0.1875
- b_proj: float32 [3584], replicated, may hold values from -3 to 3
- norm_gain: float32 [3, 3584], replicated, may hold values from 0.1 to 1.9
- w_qkv: bfloat16 [3, 3584, 2304], P(None, 'ctx', 'tp'), may hold values from -0.09375 to 0.09375
- b_qkv: float32 [3, 2304], P(None, 'tp'), may hold values from -4 to 4
- w_out: bfloat16 [3, 1792, 3584], P(None, 'tp', 'ctx'), may hold values from -1.5 to 1.5
Outputs:
- segment_out: bfloat16 [4, 8192, 3584], P('segment', 'ctx')
Inputs may be any that keep to these rules, and one draw needn't show every extreme that they name: `join`: frames never intersect; the 2 frames f with f // 2 == d lie in order inside positions d * 256 to (d + 1) * 256 - 1.
All inputs are finite; a program needn't handle non-finite values.
Results may differ from a plain program's by a relative error of at most 0.015.
Values may be sent and summed in bfloat16 or wider, within the bound.
No kernel may reach another device: no remote copies, remote signals or barrier semaphores. Data moves between devices by JAX's collectives and lax.ppermute only.
A program may use at most 128 MiB of HBM per device.

v0:
```python
from functools import partial
import jax
import jax.numpy as jnp
from jax import lax
from jax.sharding import PartitionSpec as P

HD = 128
GROUP = 7
FRAME = 64


def shifted(value, axis, by):
    devices = lax.axis_size(axis)
    pairs = [(i, i + by) for i in range(devices) if 0 <= i + by < devices]
    return lax.ppermute(value, axis, pairs)


def update_state(softmax_state, query_flat, query_pos, keys_in, values_in, offset):
    peak_old, total_old, accum_old = softmax_state
    key_pos = jnp.arange(keys_in.shape[0], dtype=jnp.int32)
    scores = jnp.dot(query_flat, keys_in.T, preferred_element_type=jnp.float32) * HD ** (-0.5)
    allowed = key_pos[None, :] <= query_pos[:, None]
    scores = jnp.where(allowed, scores, -1e30)
    peak_new = jnp.maximum(peak_old, jnp.max(scores, axis=1))
    weights = jnp.where(allowed, jnp.exp(scores - peak_new[:, None]), 0.0)
    total_new = jnp.sum(weights, axis=1)
    accum_new = jnp.dot(weights.astype(jnp.bfloat16), values_in, preferred_element_type=jnp.float32)
    return (peak_new, total_new, accum_new)


def keep_state(softmax_state):
    return softmax_state


def on_device(held, text, frames, join, ln_gain, w_proj, b_proj, norm_gain, w_qkv, b_qkv, w_out):
    segment_id = lax.axis_index("segment")
    ctx_id = lax.axis_index("ctx")
    tp_id = lax.axis_index("tp")
    hidden_in = shifted(held[0], "segment", 1)
    tok_rows = hidden_in.shape[0]
    half_rows = tok_rows // 2
    layer_id = jnp.maximum(segment_id - 1, 0)
    weight_qkv = lax.dynamic_index_in_dim(w_qkv, layer_id, 0, keepdims=False)
    bias_qkv = lax.dynamic_index_in_dim(b_qkv, layer_id, 0, keepdims=False)
    layer_gain = lax.dynamic_index_in_dim(norm_gain, layer_id, 0, keepdims=False)
    weight_out = lax.dynamic_index_in_dim(w_out, layer_id, 0, keepdims=False)
    inputs = hidden_in.astype(jnp.float32)
    normed = (
        inputs * lax.rsqrt(jnp.mean(inputs * inputs, axis=1, keepdims=True) + 1e-06) * layer_gain
    ).astype(jnp.bfloat16)
    merged = jnp.dot(
        normed,
        lax.all_gather(weight_qkv, "ctx", axis=0, tiled=True),
        preferred_element_type=jnp.float32,
    )
    merged = (merged + bias_qkv).astype(jnp.bfloat16)
    query_cols = GROUP * HD
    queries = merged[:, :query_cols]
    key_part = merged[:, query_cols : query_cols + HD]
    value_part = merged[:, query_cols + HD : query_cols + 2 * HD]
    local_steps = jnp.arange(half_rows, dtype=jnp.int32)
    first_pos = ctx_id * tok_rows + local_steps
    second_q = queries[half_rows:]
    second_pos = ctx_id * tok_rows + half_rows + local_steps
    first_flat = queries[:half_rows].reshape(half_rows * GROUP, HD)
    second_flat = second_q.reshape(half_rows * GROUP, HD)
    first_qpos = jnp.repeat(first_pos, GROUP)
    second_qpos = jnp.repeat(second_pos, GROUP)
    flat_rows = half_rows * GROUP
    empty = (
        jnp.full((flat_rows,), -1e30, jnp.float32),
        jnp.zeros((flat_rows,), jnp.float32),
        jnp.zeros((flat_rows, HD), jnp.float32),
    )
    carried = (empty, empty)
    offset = jnp.int32(0)
    keys_in = lax.all_gather(key_part, "ctx", axis=0, tiled=True)
    values_in = lax.all_gather(value_part, "ctx", axis=0, tiled=True)
    updated = []
    for softmax_state, query_flat, query_pos in (
        (carried[0], first_flat, first_qpos),
        (carried[1], second_flat, second_qpos),
    ):
        step_fn = partial(
            update_state,
            query_flat=query_flat,
            query_pos=query_pos,
            keys_in=keys_in,
            values_in=values_in,
            offset=offset,
        )
        updated.append(lax.cond(offset <= jnp.max(query_pos), step_fn, keep_state, softmax_state))

    def finish(softmax_state):
        return (
            (softmax_state[2] / softmax_state[1][:, None])
            .astype(jnp.bfloat16)
            .reshape(half_rows, GROUP * HD)
        )

    first_out = finish(updated[0])
    second_out = finish(updated[1])
    attended = jnp.concatenate([first_out, second_out], axis=0)
    partial_model = jnp.dot(
        attended,
        lax.all_gather(weight_out, "ctx", axis=1, tiled=True),
        preferred_element_type=jnp.float32,
    )
    positions = ctx_id * tok_rows + jnp.arange(tok_rows, dtype=jnp.int32)[:, None]
    starts = join[None, :]
    inside = (positions >= starts) & (positions < starts + FRAME)
    frame_base = (jnp.arange(join.shape[0], dtype=jnp.int32) * FRAME)[None, :]
    source = jnp.sum(jnp.where(inside, frame_base + positions - starts, 0), axis=1)
    is_vision = jnp.any(inside, axis=1)

    def vision_term():
        frame_in = frames.astype(jnp.float32)
        center = jnp.mean(frame_in, axis=1, keepdims=True)
        spread = jnp.mean((frame_in - center) * (frame_in - center), axis=1, keepdims=True)
        normed_frames = ((frame_in - center) * lax.rsqrt(spread + 1e-06) * ln_gain).astype(
            jnp.bfloat16
        )
        vis_width = w_proj.shape[0]
        normed_half = lax.dynamic_slice_in_dim(normed_frames, tp_id * vis_width, vis_width, 1)
        projected = jnp.dot(normed_half, w_proj, preferred_element_type=jnp.float32)
        return jnp.where(is_vision[:, None], jnp.take(projected, source, axis=0), 0.0)

    def model_term():
        return partial_model

    is_first = segment_id == 0
    section_term = lax.cond(is_first, vision_term, model_term)
    baseline = jnp.where(
        is_first, jnp.where(is_vision[:, None], b_proj[None, :], text.astype(jnp.float32)), inputs
    )
    summed = lax.psum(section_term.astype(jnp.bfloat16), "tp").astype(jnp.float32)
    result = (baseline + summed).astype(jnp.bfloat16)
    return result[None]


def solution(mesh):
    return jax.shard_map(
        on_device,
        mesh=mesh,
        in_specs=(
            P("segment", "ctx", None),
            P("ctx", None),
            P("ctx", None),
            P("ctx"),
            P(),
            P("tp", None),
            P(),
            P(),
            P(None, "ctx", "tp"),
            P(None, "tp"),
            P(None, "tp", "ctx"),
        ),
        out_specs=P("segment", "ctx", None),
        check_vma=False,
    )
```

profile of v0, /device:TPU:1, one launch (start us, length us, event | category | flops | bytes accessed | tf_op | source)
XLA Modules:
  0.0 459.2 jit_solution(11434149428011326203)
XLA Ops:
  6.5 1.1 copy-done
  7.7 0.7 constant_dynamic-slice_fusion.1
  8.5 4.1 collective-permute-start
  12.6 0.7 dynamic-slice_reduce_fusion.1
  13.4 0.9 dynamic-slice_reduce_fusion
  14.2 37.2 %collective-permute-done = bf16[256,3584]{1,0:T(8,128)(2,1)S(1)} collective-permute-done((bf16[256,3584]{1,0:T(8,128)(2,1)}, bf16[256,3584]{1,0:T(8,128)(2,1)S(1)}, u32[]{:S(2)}, u32[]{:S(2)}) %collective-permute-start) | collective-permute-done | bytes 1835040 | tf_op jit(solution)/shard_map/ppermute | solution.py:15
  51.5 0.4 fusion.31
  51.9 63.3 %all-gather.11.cloned.1.call-done = bf16[1,3584,1152]{2,1,0:T(8,128)(2,1)} async-done(((bf16[1,112,1152]{2,1,0:T(8,128)(2,1)}), bf16[1,3584,1152]{2,1,0:T(8,128)(2,1)}) %all-gather.11.cloned.1.call-update) | async-done | bytes 8257552 | tf_op jit(solution)/shard_map/all_gather | solution.py:53
  115.3 5.9 %fusion.37 = bf16[256,1152]{1,0:T(8,128)(2,1)S(1)} fusion(bf16[1,3584,1152]{2,1,0:T(8,128)(2,1)} %all-gather.11.cloned.1.call-done, bf16[256,3584]{1,0:T(8,128)(2,1)S(1)} %collective-permute-done, f32[3584]{0:T(1024)S(1)} %dynamic-slice_reduce_fusion, f32[256]{0:T(256)S(1)} %add_rsqrt_fusion.1, f32[1152]{0:T(1024)S(1)} %dynamic-slice_reduce_fusion.1), kind=kOutput, calls=%fused_computation.56 | convolution fusion | flops 2118189056 | bytes 10702336 | tf_op jit(solution)/shard_map/dot_general | solution.py:51
  121.2 0.6 fusion.49
  121.9 0.7 all-gather.9.cloned.1.call-update
  122.7 1.6 constant_dynamic-slice_fusion
  124.4 0.7 broadcast_reduce_fusion.1
  125.7 0.7 broadcast_reduce_fusion
  127.2 71.2 %all-gather.7.cloned.1.call-done = bf16[8192,128]{1,0:T(8,128)(2,1)} async-done(((bf16[256,128]{1,0:T(8,128)(2,1)}), bf16[8192,128]{1,0:T(8,128)(2,1)}) %all-gather.7.cloned.1.call-update) | async-done | bytes 2097168 | tf_op jit(solution)/shard_map/all_gather | solution.py:77
  198.4 79.4 %all-gather.9.cloned.1.call-done = bf16[8192,128]{1,0:T(8,128)(2,1)} async-done(((bf16[256,128]{1,0:T(8,128)(2,1)}), bf16[8192,128]{1,0:T(8,128)(2,1)}) %all-gather.9.cloned.1.call-update) | async-done | bytes 2097168 | tf_op jit(solution)/shard_map/all_gather | solution.py:78
  277.8 42.2 %conditional.3 = (f32[896]{0:T(1024)S(1)}, f32[896,128]{1,0:T(8,128)S(1)}) conditional(s32[]{:T(128)} %convert_element_type.51, () %tuple.27, (s32[128,7]{1,0:T(8,128)S(1)}, bf16[256,1152]{1,0:T(8,128)(2,1)S(1)}, bf16[8192,128]{1,0:T(8,128)(2,1)}, bf16[8192,128]{1,0:T(8,128)(2,1)}) %tuple.28), branch_computations={%region_3.4_spmd, %region_4.7_spmd} | conditional | flops 3875535872 | bytes 102308392 | solution.py:92
  278.3 14.2 %fusion = (f32[896]{0:T(1024)S(1)}, f32[896,8192]{1,0:T(8,128)}) fusion(s32[896]{0:T(1024)S(1)} %le.30, bf16[896,128]{1,0:T(8,128)(2,1)S(1)} %reshape.63, bf16[8192,128]{1,0:T(8,128)(2,1)} %get-tuple-element.43), kind=kOutput, calls=%fused_computation.4 | convolution fusion | flops 1908407424 | bytes 31693824 | tf_op jit(solution)/shard_map/cond/branch_1_fun/dot_general | solution.py:21
  292.5 13.1 %fusion.3 = f32[896,128]{1,0:T(8,128)S(1)} fusion(bf16[8192,128]{1,0:T(8,128)(2,1)S(1)} %copy-done.7, f32[896,8192]{1,0:T(8,128)} %get-tuple-element.86, f32[896]{0:T(1024)S(1)} %broadcast_maximum_fusion, s32[896]{0:T(1024)S(1)} %le.30), kind=kOutput, calls=%fused_computation.7 | convolution fusion | flops 1923088384 | bytes 31923200 | tf_op jit(solution)/shard_map/cond/branch_1_fun/dot_general | solution.py:27
  305.6 14.4 %fusion.2 = f32[896]{0:T(1024)S(1)} fusion(f32[896,8192]{1,0:T(8,128)} %get-tuple-element.86, f32[896]{0:T(1024)S(1)} %broadcast_maximum_fusion, s32[896]{0:T(1024)S(1)} %le.30), kind=kLoop, calls=%fused_computation.6 | loop fusion | flops 44039296 | bytes 29370880 | tf_op jit(solution)/shard_map/cond/branch_1_fun/reduce_sum | solution.py:26
  320.6 42.8 %conditional.4 = (f32[896]{0:T(1024)S(1)}, f32[896,128]{1,0:T(8,128)S(1)}) conditional(s32[]{:T(128)} %convert_element_type.55, () %tuple.29, (s32[128,7]{1,0:T(8,128)S(1)}, bf16[256,1152]{1,0:T(8,128)(2,1)S(1)}, bf16[8192,128]{1,0:T(8,128)(2,1)}, bf16[8192,128]{1,0:T(8,128)(2,1)}) %tuple.30), branch_computations={%region_8.9_spmd, %region_9.12_spmd} | conditional | flops 3875535872 | bytes 102308392 | solution.py:92
  321.3 14.4 %fusion.8 = (f32[896]{0:T(1024)S(1)}, f32[896,8192]{1,0:T(8,128)}) fusion(s32[896]{0:T(1024)S(1)} %le.38, bf16[896,128]{1,0:T(8,128)(2,1)S(1)} %reshape.64, bf16[8192,128]{1,0:T(8,128)(2,1)} %get-tuple-element.47), kind=kOutput, calls=%fused_computation.15 | convolution fusion | flops 1908407424 | bytes 31693824 | tf_op jit(solution)/shard_map/cond/branch_1_fun/dot_general | solution.py:21
  335.7 13.0 %fusion.11 = f32[896,128]{1,0:T(8,128)S(1)} fusion(bf16[8192,128]{1,0:T(8,128)(2,1)S(1)} %copy-done.8, f32[896,8192]{1,0:T(8,128)} %get-tuple-element.88, f32[896]{0:T(1024)S(1)} %broadcast_maximum_fusion.1, s32[896]{0:T(1024)S(1)} %le.38), kind=kOutput, calls=%fused_computation.18 | convolution fusion | flops 1923088384 | bytes 31923200 | tf_op jit(solution)/shard_map/cond/branch_1_fun/dot_general | solution.py:27
  348.8 14.6 %fusion.10 = f32[896]{0:T(1024)S(1)} fusion(f32[896,8192]{1,0:T(8,128)} %get-tuple-element.88, f32[896]{0:T(1024)S(1)} %broadcast_maximum_fusion.1, s32[896]{0:T(1024)S(1)} %le.38), kind=kLoop, calls=%fused_computation.17 | loop fusion | flops 44039296 | bytes 29370880 | tf_op jit(solution)/shard_map/cond/branch_1_fun/reduce_sum | solution.py:26
  363.8 7.7 %all-gather.13.cloned.1.call-done = bf16[1,896,3584]{1,2,0:T(8,128)(2,1)} async-done(((bf16[1,896,112]{1,2,0:T(8,128)(2,1)}), bf16[1,896,3584]{1,2,0:T(8,128)(2,1)}) %all-gather.13.cloned.1.call-update) | async-done | bytes 6422544 | tf_op jit(solution)/shard_map/all_gather | solution.py:106
  371.6 6.2 %fusion.27 = bf16[256,3584]{1,0:T(8,128)(2,1)} fusion(bf16[1,896,3584]{1,2,0:T(8,128)(2,1)} %all-gather.13.cloned.1.call-done, bf16[128,896]{1,0:T(8,128)(2,1)S(1)} %reshape.68, bf16[128,896]{1,0:T(8,128)(2,1)S(1)} %reshape.67), kind=kOutput, calls=%fused_computation.45 | convolution fusion | flops 1645084672 | bytes 8716288 | tf_op jit(solution)/shard_map/dot_general | solution.py:104
  377.7 7.3 %conditional.5 = (bf16[256,3584]{1,0:T(8,128)(2,1)}) conditional(s32[]{:T(128)} %convert_element_type.50, bf16[256,3584]{1,0:T(8,128)(2,1)} %fusion.27, (pred[256]{0:T(512)(128)(4,1)S(1)}, pred[256,2]{0,1:T(4,128)(4,1)S(1)}, bf16[128,1024]{1,0:T(8,128)(2,1)S(1)}, f32[1024]{0:T(1024)S(1)}, s32[]{:T(128)}, /*index=5*/bf16[512,3584]{1,0:T(8,128)(2,1)}, ...), branch_computations={%region_13.14_spmd, %region_14.17_spmd} | conditional | flops 472585344 | bytes 13264226 | solution.py:132
  378.2 2.7 fusion.18
  381.0 1.7 gather_fusion
  382.8 2.2 select_select_fusion
  385.0 62.8 %all-reduce.2.cloned.1.call-done = bf16[256,3584]{1,0:T(8,128)(2,1)} async-done(((bf16[256,3584]{1,0:T(8,128)(2,1)}), bf16[256,3584]{1,0:T(8,128)(2,1)}) %all-reduce.2.cloned.1.call-update) | async-done | bytes 1835024 | tf_op jit(solution)/shard_map/psum | solution.py:136
  447.9 4.8 %fusion.41 = bf16[1,256,3584]{2,1,0:T(8,128)(2,1)} fusion(bf16[256,3584]{1,0:T(8,128)(2,1)} %all-reduce.2.cloned.1.call-done, bf16[256,3584]{1,0:T(8,128)(2,1)} %copy-done.2, bf16[256,3584]{1,0:T(8,128)(2,1)} %param.18, f32[3584]{0:T(1024)S(1)} %copy-done.4, pred[256]{0:T(512)(128)(4,1)S(1)} %get-tuple-element.83, pred[]{:T(512)S(6)} %eq.3), kind=kLoop, calls=%fused_computation.57 | loop fusion | flops 6422528 | bytes 7354625 | tf_op jit(solution)/shard_map/broadcast_in_dim | solution.py:138
  (59 shorter events, 2.9 us)
Async XLA Ops:
  6.5 1.1 copy-start
  6.5 108.7 %all-gather.11.cloned.1.call-start = ((), (), s32[]{:S(2)}) async-start(), calls=%async_computation.3 | async-start | bytes 8515584 | tf_op jit(solution)/shard_map/all_gather | solution.py:53
  8.4 190.0 %all-gather.7.cloned.1.call-start = ((), (), s32[]{:S(2)}) async-start(), calls=%async_computation | async-start | bytes 2162688 | tf_op jit(solution)/shard_map/all_gather | solution.py:77
  8.5 43.0 %collective-permute-start = (bf16[256,3584]{1,0:T(8,128)(2,1)}, bf16[256,3584]{1,0:T(8,128)(2,1)S(1)}, u32[]{:S(2)}, u32[]{:S(2)}) collective-permute-start(bf16[256,3584]{1,0:T(8,128)(2,1)} %bitcast.20), channel_id=1, source_target_pairs={{0,64},{64,128},{128,192},{1,65},{65,129},{129,193},{2,66},{66,130... | collective-permute-start | bytes 5505032 | tf_op jit(solution)/shard_map/ppermute | solution.py:15
  51.5 69.7 %copy-start.2 = (bf16[256,3584]{1,0:T(8,128)(2,1)}, bf16[256,3584]{1,0:T(8,128)(2,1)S(1)}, u32[]{:S(2)}) copy-start(bf16[256,3584]{1,0:T(8,128)(2,1)S(1)} %collective-permute-done) | copy-start | bytes 5505028
  51.9 75.1 %copy-start.5 = (s32[2]{0:T(128)S(1)}, s32[2]{0:T(128)}, u32[]{:S(2)}) copy-start(s32[2]{0:T(128)} %param.20) | copy-start | bytes 28
  121.9 155.9 %all-gather.9.cloned.1.call-start = ((), (), s32[]{:S(2)}) async-start(), calls=%async_computation.1 | async-start | bytes 2162688 | tf_op jit(solution)/shard_map/all_gather | solution.py:78
  122.6 248.9 %all-gather.13.cloned.1.call-start = ((), (), s32[]{:S(2)}) async-start(), calls=%async_computation.4 | async-start | bytes 6623232 | tf_op jit(solution)/shard_map/all_gather | solution.py:106
  124.3 323.5 %all-reduce.2.cloned.1.call-start = ((), (), s32[]{:S(2)}) async-start(), calls=%async_computation.2 | async-start | bytes 3670016 | tf_op jit(solution)/shard_map/psum | solution.py:136
  278.3 14.2 %copy-start.7 = (bf16[8192,128]{1,0:T(8,128)(2,1)S(1)}, bf16[8192,128]{1,0:T(8,128)(2,1)}, u32[]{:S(2)}) copy-start(bf16[8192,128]{1,0:T(8,128)(2,1)} %get-tuple-element.44) | copy-start | bytes 6291460 | tf_op jit(solution)/shard_map/cond
  320.6 51.0 %copy-start.3 = (bf16[128,1024]{1,0:T(8,128)(2,1)S(1)}, bf16[128,1024]{1,0:T(8,128)(2,1)}, u32[]{:S(2)}) copy-start(bf16[128,1024]{1,0:T(8,128)(2,1)} %param.19) | copy-start | bytes 786436
  320.6 51.0 %copy-start.6 = (f32[1024]{0:T(1024)S(1)}, f32[1024]{0:T(1024)}, u32[]{:S(2)}) copy-start(f32[1024]{0:T(1024)} %param.21) | copy-start | bytes 12292
  321.3 14.4 %copy-start.8 = (bf16[8192,128]{1,0:T(8,128)(2,1)S(1)}, bf16[8192,128]{1,0:T(8,128)(2,1)}, u32[]{:S(2)}) copy-start(bf16[8192,128]{1,0:T(8,128)(2,1)} %get-tuple-element.48) | copy-start | bytes 6291460 | tf_op jit(solution)/shard_map/cond
  377.7 70.1 %copy-start.4 = (f32[3584]{0:T(1024)S(1)}, f32[3584]{0:T(1024)}, u32[]{:S(2)}) copy-start(f32[3584]{0:T(1024)} %param.23) | copy-start | bytes 43012
  385.0 67.6 %copy-start.1 = (bf16[3,112,1152]{2,1,0:T(8,128)(2,1)S(1)}, bf16[3,112,1152]{2,1,0:T(8,128)(2,1)}, u32[]{:S(2)}) copy-start(bf16[3,112,1152]{2,1,0:T(8,128)(2,1)} %param.25) | copy-start | bytes 2322436
Sparse Core Ops, SparseCore 0:
  10.0 105.1 all-gather.10
  122.0 76.3 all-gather.6
  201.2 76.5 all-gather.8
  280.3 91.2 all-gather.12
  385.2 62.6 all-reduce.1
where the time goes:
time: 460 us; the launch traced here: 459 us
  waiting for transfers between devices  322 us (70%)
  matrix products  69.6 us (15%)
  other arithmetic  38.9 us (8%)
  between operations  14.4 us (3%)
  local copies, waits for them, and re-layouts  9.21 us (2%)
    all_gather x1, waiting for transfers between devices, on_device(): values_in = lax.all_gather(value_part, 'ctx', axis=0, tiled=True)  79.4 us
    all_gather x1, waiting for transfers between devices, on_device(): keys_in = lax.all_gather(key_part, 'ctx', axis=0, tiled=True)  71.2 us
    all_gather x1, waiting for transfers between devices, on_device(): lax.all_gather(weight_qkv, 'ctx', axis=0, tiled=True)  63.3 us
    psum x1, waiting for transfers between devices, on_device(): lax.psum(section_term.astype(jnp.bfloat16), 'tp').astype(jnp.float32)  62.8 us
    ppermute x1, waiting for transfers between devices, shifted(): return lax.ppermute(value, axis, pairs)  37.2 us
    reduce_sum x2, other arithmetic, update_state(): total_new = jnp.sum(weights, axis=1)  29.1 us
    dot_general x2, matrix products, update_state(): jnp.dot(query_flat, keys_in.T, preferred_element_type=jnp.float32)  28.6 us
    dot_general x2, matrix products, update_state(): jnp.dot(weights.astype(jnp.bfloat16), values_in, preferred_element_type=j...  26.1 us
  transfers between devices with their start and end apart: 6, of which 6 were waited for; matrix products, arithmetic and copies ran while one was open for 20% of the time, Pallas kernels for 0%

commit v1 on v0

--- a/solution.py
+++ b/solution.py
@@ -74,7 +74,14 @@
     )
     carried = (empty, empty)
     offset = jnp.int32(0)
-    keys_in = lax.all_gather(key_part, "ctx", axis=0, tiled=True)
+
+    def build_frame(block_here):
+        after = jnp.stack([block_here for _ in range(lax.psum(1, "ctx"))])
+        outcome_arr = lax.all_to_all(after, "ctx", 0, 0)
+        tall = jnp.concatenate(outcome_arr, axis=0)
+        return tall
+
+    keys_in = build_frame(key_part)
     values_in = lax.all_gather(value_part, "ctx", axis=0, tiled=True)
     updated = []
     for softmax_state, query_flat, query_pos in (

time: 460 us -> 393 us (0.85)
  waiting for transfers between devices: 322 us -> 248 us
    all_gather x1 -> x0, waiting for transfers between devices: 71.2 us -> none  [on_device(): keys_in = lax.all_gather(key_part, 'ctx', axis=0, tiled=True)]
    all_gather x1, waiting for transfers between devices: 79.4 us -> 23.5 us  [on_device(): values_in = lax.all_gather(value_part, 'ctx', axis=0, tiled=True)]
    all_to_all x0 -> x1, waiting for transfers between devices: none -> 51.3 us  [build_frame(): outcome_arr = lax.all_to_all(after, 'ctx', 0, 0)]
  transfers between devices with their start and end apart: 6 -> 6, of which waited for: 6 -> 6; matrix products, arithmetic and copies ran while one was open for 20% -> 23% of each run, Pallas kernels for 0% -> 0%
where the time goes in v1:
time: 393 us; the launch traced here: 392 us
  waiting for transfers between devices  248 us (63%)
  matrix products  67.6 us (17%)
  other arithmetic  39 us (10%)
  between operations  14.5 us (4%)
  local copies, waits for them, and re-layouts  13.8 us (4%)
  starting transfers between devices  8.64 us (2%)
    all_gather x1, waiting for transfers between devices, on_device(): lax.all_gather(weight_qkv, 'ctx', axis=0, tiled=True)  63.3 us
    psum x1, waiting for transfers between devices, on_device(): lax.psum(section_term.astype(jnp.bfloat16), 'tp').astype(jnp.float32)  62.9 us
    all_to_all x1, waiting for transfers between devices, build_frame(): outcome_arr = lax.all_to_all(after, 'ctx', 0, 0)  51.3 us
    ppermute x1, waiting for transfers between devices, shifted(): return lax.ppermute(value, axis, pairs)  37.2 us
    reduce_sum x2, other arithmetic, update_state(): total_new = jnp.sum(weights, axis=1)  29.1 us
    dot_general x2, matrix products, update_state(): jnp.dot(weights.astype(jnp.bfloat16), values_in, preferred_element_type=j...  26.1 us
    dot_general x2, matrix products, update_state(): jnp.dot(query_flat, keys_in.T, preferred_element_type=jnp.float32)  25.8 us
    all_gather x1, waiting for transfers between devices, on_device(): values_in = lax.all_gather(value_part, 'ctx', axis=0, tiled=True)  23.5 us
  transfers between devices with their start and end apart: 6, of which 6 were waited for; matrix products, arithmetic and copies ran while one was open for 23% of the time, Pallas kernels for 0%

profile of v1, /device:TPU:1, one launch (start us, length us, event | category | flops | bytes accessed | tf_op | source)
XLA Modules:
  0.0 391.9 jit_solution(2587796702158688031)
XLA Ops:
  6.5 1.1 copy-done
  8.5 4.1 %collective-permute-start = (bf16[256,3584]{1,0:T(8,128)(2,1)}, bf16[256,3584]{1,0:T(8,128)(2,1)S(1)}, u32[]{:S(2)}, u32[]{:S(2)}) collective-permute-start(bf16[256,3584]{1,0:T(8,128)(2,1)} %bitcast.23), channel_id=1, source_target_pairs={{0,64},{64,128},{128,192},{1,65},{65,129},{129,193},{2,66},{66,130... | collective-permute-start | bytes 5505032 | tf_op jit(solution)/shard_map/ppermute | solution.py:15
  12.6 0.7 dynamic-slice_reduce_fusion.1
  13.4 0.9 dynamic-slice_reduce_fusion
  14.2 37.2 %collective-permute-done = bf16[256,3584]{1,0:T(8,128)(2,1)S(1)} collective-permute-done((bf16[256,3584]{1,0:T(8,128)(2,1)}, bf16[256,3584]{1,0:T(8,128)(2,1)S(1)}, u32[]{:S(2)}, u32[]{:S(2)}) %collective-permute-start) | collective-permute-done | bytes 1835040 | tf_op jit(solution)/shard_map/ppermute | solution.py:15
  51.9 63.3 %all-gather.8.cloned.1.call-done = bf16[1,3584,1152]{2,1,0:T(8,128)(2,1)} async-done(((bf16[1,112,1152]{2,1,0:T(8,128)(2,1)}), bf16[1,3584,1152]{2,1,0:T(8,128)(2,1)}) %all-gather.8.cloned.1.call-update) | async-done | bytes 8257552 | tf_op jit(solution)/shard_map/all_gather | solution.py:53
  115.3 6.8 %fusion.37 = bf16[256,1152]{1,0:T(8,128)(2,1)} fusion(bf16[1,3584,1152]{2,1,0:T(8,128)(2,1)} %all-gather.8.cloned.1.call-done, bf16[256,3584]{1,0:T(8,128)(2,1)S(1)} %collective-permute-done, f32[3584]{0:T(1024)S(1)} %dynamic-slice_reduce_fusion, f32[256]{0:T(256)S(1)} %add_rsqrt_fusion.1, f32[1152]{0:T(1024)S(1)} %dynamic-slice_reduce_fusion.1), kind=kOutput, calls=%fused_computation.56 | convolution fusion | flops 2118189056 | bytes 10702336 | tf_op jit(solution)/shard_map/dot_general | solution.py:51
  122.0 1.5 fusion.49
  123.6 1.6 constant_dynamic-slice_fusion
  125.3 1.8 stack.2
  127.1 4.4 %all-to-all-start = ((bf16[32,256,128]{2,1,0:T(8,128)(2,1)}), bf16[32,256,128]{2,1,0:T(8,128)(2,1)S(1)}, u32[]{:S(2)}, u32[]{:S(2)}) async-start(bf16[32,256,128]{2,1,0:T(8,128)(2,1)} %stack.2), calls=%async_computation | async-start | bytes 4194304 | tf_op jit(solution)/shard_map/all_to_all | solution.py:80
  131.5 0.8 broadcast_reduce_fusion.1
  134.5 51.3 %all-to-all-done = bf16[32,256,128]{2,1,0:T(8,128)(2,1)S(1)} async-done(((bf16[32,256,128]{2,1,0:T(8,128)(2,1)}), bf16[32,256,128]{2,1,0:T(8,128)(2,1)S(1)}, u32[]{:S(2)}, u32[]{:S(2)}) %all-to-all-start) | async-done | bytes 2097184 | tf_op jit(solution)/shard_map/all_to_all | solution.py:80
  185.8 23.5 %all-gather.6.cloned.1.call-done = bf16[8192,128]{1,0:T(8,128)(2,1)} async-done(((bf16[256,128]{1,0:T(8,128)(2,1)}), bf16[8192,128]{1,0:T(8,128)(2,1)}) %all-gather.6.cloned.1.call-update) | async-done | bytes 2097168 | tf_op jit(solution)/shard_map/all_gather | solution.py:85
  209.4 41.9 %conditional.3 = (f32[896]{0:T(1024)S(1)}, f32[896,128]{1,0:T(8,128)S(1)}) conditional(s32[]{:T(128)} %convert_element_type.51, () %tuple.27, (s32[128,7]{1,0:T(8,128)S(1)}, bf16[256,1152]{1,0:T(8,128)(2,1)}, bf16[8192,128]{1,0:T(8,128)(2,1)S(1)}, bf16[8192,128]{1,0:T(8,128)(2,1)}) %tuple.51), branch_computations={%region_3.4_spmd, %region_4.7_spmd} | conditional | flops 3875535872 | bytes 102308392 | solution.py:99
  209.6 1.0 slice.13
  210.8 12.8 %fusion = (f32[896]{0:T(1024)S(1)}, f32[896,8192]{1,0:T(8,128)}) fusion(s32[896]{0:T(1024)S(1)} %le.30, bf16[896,128]{1,0:T(8,128)(2,1)S(1)} %reshape.67, bf16[8192,128]{1,0:T(8,128)(2,1)S(1)} %get-tuple-element.43), kind=kOutput, calls=%fused_computation.4 | convolution fusion | flops 1908407424 | bytes 31693824 | tf_op jit(solution)/shard_map/cond/branch_1_fun/dot_general | solution.py:21
  223.6 13.1 %fusion.3 = f32[896,128]{1,0:T(8,128)S(1)} fusion(bf16[8192,128]{1,0:T(8,128)(2,1)S(1)} %copy-done.7, f32[896,8192]{1,0:T(8,128)} %get-tuple-element.86, f32[896]{0:T(1024)S(1)} %broadcast_maximum_fusion, s32[896]{0:T(1024)S(1)} %le.30), kind=kOutput, calls=%fused_computation.7 | convolution fusion | flops 1923088384 | bytes 31923200 | tf_op jit(solution)/shard_map/cond/branch_1_fun/dot_general | solution.py:27
  236.7 14.5 %fusion.2 = f32[896]{0:T(1024)S(1)} fusion(f32[896,8192]{1,0:T(8,128)} %get-tuple-element.86, f32[896]{0:T(1024)S(1)} %broadcast_maximum_fusion, s32[896]{0:T(1024)S(1)} %le.30), kind=kLoop, calls=%fused_computation.6 | loop fusion | flops 44039296 | bytes 29370880 | tf_op jit(solution)/shard_map/cond/branch_1_fun/reduce_sum | solution.py:26
  251.9 42.2 %conditional.4 = (f32[896]{0:T(1024)S(1)}, f32[896,128]{1,0:T(8,128)S(1)}) conditional(s32[]{:T(128)} %convert_element_type.55, () %tuple.29, (s32[128,7]{1,0:T(8,128)S(1)}, bf16[256,1152]{1,0:T(8,128)(2,1)}, bf16[8192,128]{1,0:T(8,128)(2,1)S(1)}, bf16[8192,128]{1,0:T(8,128)(2,1)}) %tuple.52), branch_computations={%region_8.9_spmd, %region_9.12_spmd} | conditional | flops 3875535872 | bytes 102308392 | solution.py:99
  252.1 1.0 slice.14
  253.3 13.0 %fusion.8 = (f32[896]{0:T(1024)S(1)}, f32[896,8192]{1,0:T(8,128)}) fusion(s32[896]{0:T(1024)S(1)} %le.38, bf16[896,128]{1,0:T(8,128)(2,1)S(1)} %reshape.68, bf16[8192,128]{1,0:T(8,128)(2,1)S(1)} %get-tuple-element.47), kind=kOutput, calls=%fused_computation.15 | convolution fusion | flops 1908407424 | bytes 31693824 | tf_op jit(solution)/shard_map/cond/branch_1_fun/dot_general | solution.py:21
  266.3 13.1 %fusion.11 = f32[896,128]{1,0:T(8,128)S(1)} fusion(bf16[8192,128]{1,0:T(8,128)(2,1)S(1)} %copy-done.8, f32[896,8192]{1,0:T(8,128)} %get-tuple-element.88, f32[896]{0:T(1024)S(1)} %broadcast_maximum_fusion.1, s32[896]{0:T(1024)S(1)} %le.38), kind=kOutput, calls=%fused_computation.18 | convolution fusion | flops 1923088384 | bytes 31923200 | tf_op jit(solution)/shard_map/cond/branch_1_fun/dot_general | solution.py:27
  279.4 14.6 %fusion.10 = f32[896]{0:T(1024)S(1)} fusion(f32[896,8192]{1,0:T(8,128)} %get-tuple-element.88, f32[896]{0:T(1024)S(1)} %broadcast_maximum_fusion.1, s32[896]{0:T(1024)S(1)} %le.38), kind=kLoop, calls=%fused_computation.17 | loop fusion | flops 44039296 | bytes 29370880 | tf_op jit(solution)/shard_map/cond/branch_1_fun/reduce_sum | solution.py:26
  294.5 9.8 %all-gather.10.cloned.1.call-done = bf16[1,896,3584]{1,2,0:T(8,128)(2,1)} async-done(((bf16[1,896,112]{1,2,0:T(8,128)(2,1)}), bf16[1,896,3584]{1,2,0:T(8,128)(2,1)}) %all-gather.10.cloned.1.call-update) | async-done | bytes 6422544 | tf_op jit(solution)/shard_map/all_gather | solution.py:113
  304.3 6.2 %fusion.27 = bf16[256,3584]{1,0:T(8,128)(2,1)} fusion(bf16[1,896,3584]{1,2,0:T(8,128)(2,1)} %all-gather.10.cloned.1.call-done, bf16[128,896]{1,0:T(8,128)(2,1)S(1)} %reshape.74, bf16[128,896]{1,0:T(8,128)(2,1)S(1)} %reshape.73), kind=kOutput, calls=%fused_computation.45 | convolution fusion | flops 1645084672 | bytes 8716288 | tf_op jit(solution)/shard_map/dot_general | solution.py:111
  310.4 7.3 %conditional.5 = (bf16[256,3584]{1,0:T(8,128)(2,1)}) conditional(s32[]{:T(128)} %convert_element_type.50, bf16[256,3584]{1,0:T(8,128)(2,1)} %fusion.27, (pred[256]{0:T(512)(128)(4,1)S(1)}, pred[256,2]{0,1:T(4,128)(4,1)S(1)}, bf16[128,1024]{1,0:T(8,128)(2,1)S(1)}, f32[1024]{0:T(1024)S(1)}, s32[]{:T(128)}, /*index=5*/bf16[512,3584]{1,0:T(8,128)(2,1)}, ...), branch_computations={%region_13.14_spmd, %region_14.17_spmd} | conditional | flops 472585344 | bytes 13264226 | solution.py:139
  310.9 2.7 fusion.18
  313.7 1.7 gather_fusion
  315.5 2.2 select_select_fusion
  317.7 62.9 %all-reduce.2.cloned.1.call-done = bf16[256,3584]{1,0:T(8,128)(2,1)} async-done(((bf16[256,3584]{1,0:T(8,128)(2,1)}), bf16[256,3584]{1,0:T(8,128)(2,1)}) %all-reduce.2.cloned.1.call-update) | async-done | bytes 1835024 | tf_op jit(solution)/shard_map/psum | solution.py:143
  380.6 4.8 %fusion.41 = bf16[1,256,3584]{2,1,0:T(8,128)(2,1)} fusion(bf16[256,3584]{1,0:T(8,128)(2,1)} %all-reduce.2.cloned.1.call-done, bf16[256,3584]{1,0:T(8,128)(2,1)} %copy-done.2, bf16[256,3584]{1,0:T(8,128)(2,1)} %param.18, f32[3584]{0:T(1024)S(1)} %copy-done.4, pred[256]{0:T(512)(128)(4,1)S(1)} %get-tuple-element.83, pred[]{:T(512)S(6)} %eq.3), kind=kLoop, calls=%fused_computation.57 | loop fusion | flops 6422528 | bytes 7354625 | tf_op jit(solution)/shard_map/broadcast_in_dim | solution.py:145
  (59 shorter events, 4.8 us)
Async XLA Ops:
  6.5 1.1 copy-start
  6.5 108.7 %all-gather.8.cloned.1.call-start = ((), (), s32[]{:S(2)}) async-start(), calls=%async_computation.3 | async-start | bytes 8515584 | tf_op jit(solution)/shard_map/all_gather | solution.py:53
  8.4 200.9 %all-gather.6.cloned.1.call-start = ((), (), s32[]{:S(2)}) async-start(), calls=%async_computation.1 | async-start | bytes 2162688 | tf_op jit(solution)/shard_map/all_gather | solution.py:85
  8.5 43.0 %collective-permute-start = (bf16[256,3584]{1,0:T(8,128)(2,1)}, bf16[256,3584]{1,0:T(8,128)(2,1)S(1)}, u32[]{:S(2)}, u32[]{:S(2)}) collective-permute-start(bf16[256,3584]{1,0:T(8,128)(2,1)} %bitcast.23), channel_id=1, source_target_pairs={{0,64},{64,128},{128,192},{1,65},{65,129},{129,193},{2,66},{66,130... | collective-permute-start | bytes 5505032 | tf_op jit(solution)/shard_map/ppermute | solution.py:15
  51.5 70.6 %copy-start.2 = (bf16[256,3584]{1,0:T(8,128)(2,1)}, bf16[256,3584]{1,0:T(8,128)(2,1)S(1)}, u32[]{:S(2)}) copy-start(bf16[256,3584]{1,0:T(8,128)(2,1)S(1)} %collective-permute-done) | copy-start | bytes 5505028
  51.9 82.4 %copy-start.5 = (s32[2]{0:T(128)S(1)}, s32[2]{0:T(128)}, u32[]{:S(2)}) copy-start(s32[2]{0:T(128)} %param.20) | copy-start | bytes 28
  123.6 180.7 %all-gather.10.cloned.1.call-start = ((), (), s32[]{:S(2)}) async-start(), calls=%async_computation.4 | async-start | bytes 6623232 | tf_op jit(solution)/shard_map/all_gather | solution.py:113
  127.1 58.8 %all-to-all-start = ((bf16[32,256,128]{2,1,0:T(8,128)(2,1)}), bf16[32,256,128]{2,1,0:T(8,128)(2,1)S(1)}, u32[]{:S(2)}, u32[]{:S(2)}) async-start(bf16[32,256,128]{2,1,0:T(8,128)(2,1)} %stack.2), calls=%async_computation | async-start | bytes 4194304 | tf_op jit(solution)/shard_map/all_to_all | solution.py:80
  131.4 249.2 %all-reduce.2.cloned.1.call-start = ((), (), s32[]{:S(2)}) async-start(), calls=%async_computation.2 | async-start | bytes 3670016 | tf_op jit(solution)/shard_map/psum | solution.py:143
  210.8 12.8 %copy-start.7 = (bf16[8192,128]{1,0:T(8,128)(2,1)S(1)}, bf16[8192,128]{1,0:T(8,128)(2,1)}, u32[]{:S(2)}) copy-start(bf16[8192,128]{1,0:T(8,128)(2,1)} %get-tuple-element.44) | copy-start | bytes 6291460 | tf_op jit(solution)/shard_map/cond
  251.9 52.4 %copy-start.3 = (bf16[128,1024]{1,0:T(8,128)(2,1)S(1)}, bf16[128,1024]{1,0:T(8,128)(2,1)}, u32[]{:S(2)}) copy-start(bf16[128,1024]{1,0:T(8,128)(2,1)} %param.19) | copy-start | bytes 786436
  251.9 52.4 %copy-start.6 = (f32[1024]{0:T(1024)S(1)}, f32[1024]{0:T(1024)}, u32[]{:S(2)}) copy-start(f32[1024]{0:T(1024)} %param.21) | copy-start | bytes 12292
  253.3 13.0 %copy-start.8 = (bf16[8192,128]{1,0:T(8,128)(2,1)S(1)}, bf16[8192,128]{1,0:T(8,128)(2,1)}, u32[]{:S(2)}) copy-start(bf16[8192,128]{1,0:T(8,128)(2,1)} %get-tuple-element.48) | copy-start | bytes 6291460 | tf_op jit(solution)/shard_map/cond
  310.4 70.2 %copy-start.4 = (f32[3584]{0:T(1024)S(1)}, f32[3584]{0:T(1024)}, u32[]{:S(2)}) copy-start(f32[3584]{0:T(1024)} %param.23) | copy-start | bytes 43012
  317.7 67.7 %copy-start.1 = (bf16[3,112,1152]{2,1,0:T(8,128)(2,1)S(1)}, bf16[3,112,1152]{2,1,0:T(8,128)(2,1)}, u32[]{:S(2)}) copy-start(bf16[3,112,1152]{2,1,0:T(8,128)(2,1)} %param.25) | copy-start | bytes 2322436
Sparse Core Ops, SparseCore 0:
  10.0 105.1 all-gather.7
  123.7 85.5 all-gather.5
  212.0 92.2 all-gather.9
  317.9 62.7 all-reduce.1
